TPU v7x, 32 devices: a whole 2x2x4 slice. The times are simulated.
32 devices in a mesh: group: 2 (over y), head: 4 (over x, core), seq: 4 (over z).
Axes of the slice: x: 2, y: 2, z: 4, core: 2. Of those that a mesh axis runs over, the one named last changes fastest.
Arguments:
- new_queries: bfloat16 [512, 4096], P(('group', 'seq'), 'head'), parts along dimension 0, may hold values from -80 to 80
- new_keys: bfloat16 [512, 1024], P(('group', 'seq'), 'head'), parts along dimension 0, may hold values from -6 to 6
- new_values: bfloat16 [512, 1024], P(('group', 'seq'), 'head'), parts along dimension 0, may hold values from -6 to 6
- cache_keys: bfloat16 [8192, 1024], P(('group', 'seq'), 'head'), parts along dimension 0, may hold values from -5 to 5
- cache_values: bfloat16 [8192, 1024], P(('group', 'seq'), 'head'), parts along dimension 0, may hold values from -6 to 6
- segment_ids: int32 [512], P('group'), parts along dimension 0, may hold values from 0 to 7, as said below
- cache_length: int32 [2], P('group'), parts along dimension 0, may hold values from 512 to 4096
Outputs:
- attended: bfloat16 [512, 4096], P(('group', 'seq'), 'head'), parts along dimension 0
There are 2 independent parts, one for each index of `group`. A program takes and returns all parts, laid end to end along the dimension named above; each array names one. Nothing has to cross between parts.
Inputs may be any that keep to these rules, and one draw needn't show every extreme that they name: `segment_ids`: Non-decreasing along the positions; every number of 0 to 7 appears.
All inputs are finite; a program needn't handle non-finite values.
Results may differ from a plain program's by a relative error of at most 0.0024.
Values may be sent and summed in bfloat16 or wider, within the bound.
No kernel may reach another device: no remote copies, remote signals or barrier semaphores. Data moves between devices by JAX's collectives and lax.ppermute only.
A program may use at most 64 MiB of HBM per device.

v0:
```python
import jax
import jax.numpy as jnp
from jax import lax
from jax.sharding import PartitionSpec as P

HEAD_DIM = 128
NEG_FILL = -1e30


def on_device(
    new_queries, new_keys, new_values, cache_keys, cache_values, segment_ids, cache_length
):
    head_size = HEAD_DIM
    own_count = new_queries.shape[0]
    join_rows = segment_ids.shape[0]
    cache_rows = cache_keys.shape[0]
    heads_kv = cache_keys.shape[1] // head_size
    heads_q = new_queries.shape[1] // head_size
    group_size = heads_q // heads_kv
    seq_count = lax.axis_size("seq")
    seq_rank = lax.axis_index("seq")
    score_scale = head_size ** (-0.5)
    cache_limit = cache_length[0]
    all_queries, all_keys, all_values = (
        lax.all_gather(new_queries, "seq", axis=0, tiled=True),
        lax.all_gather(new_keys, "seq", axis=0, tiled=True),
        lax.all_gather(new_values, "seq", axis=0, tiled=True),
    )
    keys_here, values_here = (cache_keys, cache_values)
    live_rows = jnp.clip(cache_limit - seq_rank * cache_rows, 0, cache_rows)
    tile_width = min(cache_rows // seq_count, 256)
    block_rows = min(256, cache_rows)
    tiles_per_block = block_rows // tile_width
    block_total = (live_rows + block_rows - 1) // block_rows
    keys_tiled = keys_here.reshape(cache_rows, heads_kv, head_size)
    values_tiled = values_here.reshape(cache_rows, heads_kv, head_size)
    query_block = min(64, join_rows)
    grouped = all_queries.reshape(
        join_rows // query_block, query_block, heads_kv, group_size, head_size
    )

    def one_block(block_queries):

        def step_pass(block_index, running):
            best, numer_acc, denom_acc = running
            start = block_index * block_rows
            key_tile = lax.dynamic_slice_in_dim(keys_tiled, start, block_rows, 0)
            scores = (
                jnp.einsum(
                    "cgrd,tgd->cgrt", block_queries, key_tile, preferred_element_type=jnp.float32
                )
                * score_scale
            )
            usable = (start + jnp.arange(block_rows, dtype=jnp.int32) < live_rows).reshape(
                tiles_per_block, tile_width
            )
            split = scores.reshape(query_block, heads_kv, group_size, tiles_per_block, tile_width)
            tile_max = jnp.max(jnp.where(usable, split, NEG_FILL), axis=-1)
            weights = jnp.exp(jnp.where(usable, split - tile_max[..., None], NEG_FILL)).astype(
                jnp.bfloat16
            )
            value_tile = lax.dynamic_slice_in_dim(values_tiled, start, block_rows, 0).reshape(
                tiles_per_block, tile_width, heads_kv, head_size
            )
            tile_numer = jnp.einsum(
                "cgrbt,btgd->cgrbd", weights, value_tile, preferred_element_type=jnp.float32
            )
            tile_denom = jnp.sum(weights.astype(jnp.float32), axis=-1)
            new_best = jnp.maximum(best, jnp.max(tile_max, axis=-1))
            keep = jnp.exp(best - new_best)
            factor = jnp.exp(tile_max - new_best[..., None])
            numer_acc = numer_acc * keep[..., None] + jnp.sum(
                tile_numer * factor[..., None], axis=3
            )
            denom_acc = denom_acc * keep + jnp.sum(tile_denom * factor, axis=-1)
            return (new_best, numer_acc, denom_acc)

        start_state = (
            jnp.full((query_block, heads_kv, group_size), NEG_FILL, jnp.float32),
            jnp.zeros((query_block, heads_kv, group_size, head_size), jnp.float32),
            jnp.zeros((query_block, heads_kv, group_size), jnp.float32),
        )
        return lax.fori_loop(0, block_total, step_pass, start_state)

    block_best, block_numer, block_denom = lax.map(one_block, grouped)
    cache_max = block_best.reshape(join_rows, heads_kv, group_size)
    cache_numer = block_numer.reshape(join_rows, heads_kv, group_size, head_size)
    cache_denom = block_denom.reshape(join_rows, heads_kv, group_size)
    own_queries = new_queries.reshape(own_count, heads_kv, group_size, head_size)
    fresh_scores = (
        jnp.einsum(
            "cgrd,tgd->cgrt",
            own_queries,
            all_keys.reshape(join_rows, heads_kv, head_size),
            preferred_element_type=jnp.float32,
        )
        * score_scale
    )
    start_row = seq_rank * own_count
    own_positions = start_row + jnp.arange(own_count, dtype=jnp.int32)
    own_segments = lax.dynamic_slice_in_dim(segment_ids, start_row, own_count, 0)
    key_positions = jnp.arange(join_rows, dtype=jnp.int32)
    allowed = (key_positions[None, :] <= own_positions[:, None]) & (
        segment_ids[None, :] == own_segments[:, None]
    )
    allowed = allowed[:, None, None, :]
    fresh_max = jnp.max(jnp.where(allowed, fresh_scores, NEG_FILL), axis=-1)
    zero_index = jnp.zeros((), jnp.int32)
    merged = lax.dynamic_update_slice(
        cache_max,
        jnp.maximum(lax.dynamic_slice_in_dim(cache_max, start_row, own_count, 0), fresh_max),
        (start_row, zero_index, zero_index),
    )
    row_max = (
        lax.pmax(merged.reshape(join_rows, heads_q).astype(jnp.bfloat16), "seq")
        .astype(jnp.float32)
        .reshape(join_rows, heads_kv, group_size)
    )
    rescale = jnp.exp(cache_max - row_max)
    scaled_numer = (cache_numer * rescale[..., None]).reshape(join_rows, heads_q * head_size)
    scaled_denom = (cache_denom * rescale).reshape(join_rows, heads_q)
    own_numer, own_denom = (
        lax.psum_scatter(scaled_numer, "seq", scatter_dimension=0, tiled=True),
        lax.psum_scatter(scaled_denom, "seq", scatter_dimension=0, tiled=True),
    )
    own_max = lax.dynamic_slice_in_dim(row_max, start_row, own_count, 0)
    fresh_weights = jnp.exp(
        jnp.where(allowed, fresh_scores - fresh_max[..., None], NEG_FILL)
    ).astype(jnp.bfloat16)
    fresh_factor = jnp.exp(fresh_max - own_max)
    fresh_numer = (
        jnp.einsum(
            "cgrt,tgd->cgrd",
            fresh_weights,
            all_values.reshape(join_rows, heads_kv, head_size),
            preferred_element_type=jnp.float32,
        )
        * fresh_factor[..., None]
    )
    fresh_denom = jnp.sum(fresh_weights.astype(jnp.float32), axis=-1) * fresh_factor
    total_numer = own_numer + fresh_numer.reshape(own_count, heads_q * head_size)
    total_denom = own_denom + fresh_denom.reshape(own_count, heads_q)
    attended = total_numer.reshape(own_count, heads_q, head_size) / total_denom[..., None]
    return attended.reshape(own_count, heads_q * head_size).astype(jnp.bfloat16)


def solution(mesh):
    placed = (
        P(("group", "seq"), "head"),
        P(("group", "seq"), "head"),
        P(("group", "seq"), "head"),
        P(("group", "seq"), "head"),
        P(("group", "seq"), "head"),
        P("group"),
        P("group"),
    )
    return jax.shard_map(
        on_device,
        mesh=mesh,
        in_specs=placed,
        out_specs=P(("group", "seq"), "head"),
        check_vma=False,
    )
```

profile of v0, /device:TPU:0, one launch (start us, length us, event | category | flops | bytes accessed | tf_op | source)
XLA Modules:
  0.0 127.6 jit_solution(12809682222911493052)
XLA Ops:
  7.2 17.6 %all_gather.9 = bf16[256,1024]{1,0:T(8,128)(2,1)S(1)} all-gather(bf16[64,1024]{1,0:T(8,128)(2,1)} %param.11), channel_id=1, replica_groups=mesh['group'=2,'head'=4,'seq'=4] {'seq'}, dimensions={0}, use_global_device_ids=true | all-gather | bytes 655360 | tf_op jit(solution)/shard_map/all_gather | solution.py:25
  24.8 0.4 reshape.144
  25.2 0.7 copy-done.1
  26.3 1.3 copy.30
  27.9 18.3 %while.29 = (s32[]{:T(128)}, f32[4,64,2,4]{1,0,3,2:T(4,128)S(1)}, f32[4,64,2,4,128]{4,3,2,1,0:T(4,128)S(1)}, f32[4,64,2,4]{1,0,3,2:T(4,128)S(1)}, bf16[4,64,2,4,...) while((s32[]{:T(128)}, f32[4,64,2,4]{1,0,3,2:T(4,128)S(1)}, ...), condition=%wide.region_5.6_spmd, body=%wide.region_0.5_spmd.sunk | while | flops 68749824 | bytes 3850228 | solution.py:85
  28.0 4.1 %while.30 = (s32[]{:T(128)}, f32[64,2,4]{0,2,1:T(4,128)S(1)}, f32[64,2,4,128]{3,0,2,1:T(8,128)S(1)}, f32[64,2,4]{0,2,1:T(4,128)S(1)}, s32[]{:T(128)}, /*index=5*...) while((s32[]{:T(128)}, f32[64,2,4]{0,2,1:T(4,128)S(1)}, ...), condition=%wide.region_4.4_spmd, body=%wide.region_1.3_spmd.sunk | while | flops 68749824 | bytes 2526915 | solution.py:83
  32.6 4.1 %while.30 = (s32[]{:T(128)}, f32[64,2,4]{0,2,1:T(4,128)S(1)}, f32[64,2,4,128]{3,0,2,1:T(8,128)S(1)}, f32[64,2,4]{0,2,1:T(4,128)S(1)}, s32[]{:T(128)}, /*index=5*...) while((s32[]{:T(128)}, f32[64,2,4]{0,2,1:T(4,128)S(1)}, ...), condition=%wide.region_4.4_spmd, body=%wide.region_1.3_spmd.sunk | while | flops 68749824 | bytes 2526915 | solution.py:83
  37.1 4.1 %while.30 = (s32[]{:T(128)}, f32[64,2,4]{0,2,1:T(4,128)S(1)}, f32[64,2,4,128]{3,0,2,1:T(8,128)S(1)}, f32[64,2,4]{0,2,1:T(4,128)S(1)}, s32[]{:T(128)}, /*index=5*...) while((s32[]{:T(128)}, f32[64,2,4]{0,2,1:T(4,128)S(1)}, ...), condition=%wide.region_4.4_spmd, body=%wide.region_1.3_spmd.sunk | while | flops 68749824 | bytes 2526915 | solution.py:83
  41.7 4.1 %while.30 = (s32[]{:T(128)}, f32[64,2,4]{0,2,1:T(4,128)S(1)}, f32[64,2,4,128]{3,0,2,1:T(8,128)S(1)}, f32[64,2,4]{0,2,1:T(4,128)S(1)}, s32[]{:T(128)}, /*index=5*...) while((s32[]{:T(128)}, f32[64,2,4]{0,2,1:T(4,128)S(1)}, ...), condition=%wide.region_4.4_spmd, body=%wide.region_1.3_spmd.sunk | while | flops 68749824 | bytes 2526915 | solution.py:83
  46.5 0.7 copy-done.3
  47.1 13.3 %all_gather.10 = bf16[256,256]{1,0:T(8,128)(2,1)S(1)} all-gather(bf16[64,256]{1,0:T(8,128)(2,1)S(1)} %copy-done.3), channel_id=1, replica_groups=mesh['group'=2,'head'=4,'seq'=4] {'seq'}, dimensions={0}, use_global_device_ids=true | all-gather | bytes 163840 | tf_op jit(solution)/shard_map/all_gather | solution.py:26
  60.6 0.7 copy-done.5
  62.0 8.7 %pmax.7 = bf16[256,8]{0,1:T(8,128)(2,1)S(1)} all-reduce(bf16[256,8]{0,1:T(8,128)(2,1)S(1)} %convert_element_type.27), channel_id=1, replica_groups=mesh['group'=2,'head'=4,'seq'=4] {'seq'}, use_global_device_ids=true, to_apply=%region_7.8 | all-reduce | flops 2048 | bytes 8192 | tf_op jit(solution)/shard_map/pmax | solution.py:115
  70.7 0.8 copy.54
  71.6 0.4 reshape.147
  72.2 1.6 %mul.74 = f32[256,2,4,128]{3,2,1,0:T(4,128)} broadcast(f32[256,2,4]{2,1,0:T(2,128)S(1)} %copy.39), dimensions={0,1,2} | broadcast | bytes 1056768 | tf_op jit(solution)/shard_map/mul | solution.py:120
  73.8 1.6 %mul.75 = f32[256,1024]{1,0:T(8,128)S(1)} reshape(f32[256,2,4,128]{3,2,1,0:T(4,128)} %mul.74) | data formatting | bytes 2097152 | tf_op jit(solution)/shard_map/mul | solution.py:120
  75.4 1.2 mul.76
  76.6 0.7 copy-done.4
  77.3 13.5 %all_gather.11 = bf16[256,256]{1,0:T(8,128)(2,1)S(1)} all-gather(bf16[64,256]{1,0:T(8,128)(2,1)S(1)} %copy-done.4), channel_id=1, replica_groups=mesh['group'=2,'head'=4,'seq'=4] {'seq'}, dimensions={0}, use_global_device_ids=true | all-gather | bytes 163840 | tf_op jit(solution)/shard_map/all_gather | solution.py:27
  92.0 0.8 copy.55
  92.9 26.2 %reduce-scatter.5.cloned.1.call-done = f32[64,1024]{1,0:T(8,128)} async-done(((f32[256,1024]{1,0:T(8,128)}), f32[64,1024]{1,0:T(8,128)}) %reduce-scatter.5.cloned.1.call-update) | async-done | bytes 262160 | tf_op jit(solution)/shard_map/reduce_scatter | solution.py:123
  119.2 0.8 copy-done.2
  120.0 0.7 fusion.13
  (157 shorter events, 20.6 us)
Async XLA Ops:
  6.5 85.4 %reduce-scatter.7.cloned.1.call-start = ((), (), s32[]{:S(2)}) async-start(), calls=%async_computation.3 | async-start | bytes 163840
  24.8 1.0 copy-start.1
  27.9 18.4 %copy-start = (bf16[64,1024]{1,0:T(8,128)(2,1)S(1)}, bf16[64,1024]{1,0:T(8,128)(2,1)}, u32[]{:S(2)}) copy-start(bf16[64,1024]{1,0:T(8,128)(2,1)} %param.11) | copy-start | bytes 393220
  46.4 0.8 copy-start.3
  60.6 0.7 copy-start.5
  71.5 47.6 %reduce-scatter.5.cloned.1.call-start = ((), (), s32[]{:S(2)}) async-start(), calls=%async_computation.2 | async-start | bytes 1310720 | tf_op jit(solution)/shard_map/reduce_scatter | solution.py:123
  76.6 0.8 copy-start.4
  119.1 0.9 copy-start.2
Sparse Core Ops, SparseCore 0:
  71.6 19.7 reduce-scatter.6
  93.8 25.1 reduce-scatter.4
where the time goes:
time: 128 us
  blocking collectives  53.1 us (41%)
  waiting for transfers between devices  26.3 us (21%)
  between operations  14.3 us (11%)
  local copies, waits for them, and re-layouts  14.1 us (11%)
  matrix products  11.4 us (9%)
  other arithmetic  7.33 us (6%)
    reduce_scatter x1, waiting for transfers between devices, on_device(): lax.psum_scatter(scaled_numer, 'seq', scatter_dimension=0, tiled=True)  26.2 us
    all_gather x1, blocking collectives, on_device(): lax.all_gather(new_queries, 'seq', axis=0, tiled=True)  17.6 us
    all_gather x1, blocking collectives, on_device(): lax.all_gather(new_values, 'seq', axis=0, tiled=True)  13.5 us
    all_gather x1, blocking collectives, on_device(): lax.all_gather(new_keys, 'seq', axis=0, tiled=True)  13.3 us
    pmax x1, blocking collectives, on_device(): lax.pmax(merged.reshape(join_rows, heads_q).astype(jnp.bfloat16), 'seq')  8.67 us
    unnamed x17, local copies, waits for them, and re-layouts  6.63 us
    dot_general x16, matrix products, step_pass(): jnp.einsum('cgrbt,btgd->cgrbd', weights, value_tile, preferred_element_ty...  5.59 us
    dot_general x16, matrix products, step_pass(): jnp.einsum('cgrd,tgd->cgrt', block_queries, key_tile, preferred_element_t...  5.24 us
  transfers between devices with their start and end apart: 2, of which 1 were waited for; matrix products, arithmetic and copies ran while one was open for 5% of the time, Pallas kernels for 0%

commit v1 on v0

--- a/solution.py
+++ b/solution.py
@@ -5,6 +5,17 @@
 
 HEAD_DIM = 128
 NEG_FILL = -1e30
+
+
+def gather_around(x, axis, dim):
+    ways = lax.axis_size(axis)
+    pieces = [x]
+    for far in range(1, ways):
+        pieces.append(
+            lax.ppermute(pieces[far - 1], axis, [(d, (d - 1) % ways) for d in range(ways)])
+        )
+    line = jnp.concatenate(pieces, axis=dim)
+    return jnp.roll(line, lax.axis_index(axis) * x.shape[dim], axis=dim)
 
 
 def on_device(
@@ -23,7 +34,7 @@
     cache_limit = cache_length[0]
     all_queries, all_keys, all_values = (
         lax.all_gather(new_queries, "seq", axis=0, tiled=True),
-        lax.all_gather(new_keys, "seq", axis=0, tiled=True),
+        gather_around(new_keys, "seq", 0),
         lax.all_gather(new_values, "seq", axis=0, tiled=True),
     )
     keys_here, values_here = (cache_keys, cache_values)

time: 128 us -> 130 us (1.016)
  blocking collectives: 53.1 us -> 42.2 us
  starting transfers between devices: 0.04 us -> 7.48 us
  waiting for transfers between devices: 26.3 us -> 29.1 us
  local copies, waits for them, and re-layouts: 14.1 us -> 16.1 us
    all_gather x1 -> x0, blocking collectives: 13.3 us -> none  [on_device(): lax.all_gather(new_keys, 'seq', axis=0, tiled=True)]
    ppermute x0 -> x3, starting transfers between devices: none -> 7.44 us  [gather_around(): lax.ppermute(pieces[far - 1], axis, [(d, (d - 1) % ways) for d in range(w...]
    ppermute x0 -> x3, waiting for transfers between devices: none -> 4.61 us  [gather_around(): lax.ppermute(pieces[far - 1], axis, [(d, (d - 1) % ways) for d in range(w...]
    pmax x1, blocking collectives: 8.67 us -> 12.8 us  [on_device(): lax.pmax(merged.reshape(join_rows, heads_q).astype(jnp.bfloat16), 'seq')]
    reduce_scatter x1, waiting for transfers between devices: 26.2 us -> 24.4 us  [on_device(): lax.psum_scatter(scaled_numer, 'seq', scatter_dimension=0, tiled=True)]
    all_gather x1, blocking collectives: 17.6 us -> 15.9 us  [on_device(): lax.all_gather(new_queries, 'seq', axis=0, tiled=True)]
    unnamed x17 -> x18, local copies, waits for them, and re-layouts: 6.63 us -> 7.49 us
  transfers between devices with their start and end apart: 2 -> 5, of which waited for: 1 -> 3; matrix products, arithmetic and copies ran while one was open for 5% -> 21% of each run, Pallas kernels for 0% -> 0%
where the time goes in v1:
time: 130 us; the launch traced here: 129 us
  blocking collectives  42.2 us (32%)
  waiting for transfers between devices  29.1 us (22%)
  local copies, waits for them, and re-layouts  16.1 us (12%)
  between operations  14.3 us (11%)
  matrix products  11.4 us (9%)
  starting transfers between devices  7.48 us (6%)
  other arithmetic  7.35 us (6%)
    reduce_scatter x1, waiting for transfers between devices, on_device(): lax.psum_scatter(scaled_numer, 'seq', scatter_dimension=0, tiled=True)  24.4 us
    all_gather x1, blocking collectives, on_device(): lax.all_gather(new_queries, 'seq', axis=0, tiled=True)  15.9 us
    all_gather x1, blocking collectives, on_device(): lax.all_gather(new_values, 'seq', axis=0, tiled=True)  13.5 us
    pmax x1, blocking collectives, on_device(): lax.pmax(merged.reshape(join_rows, heads_q).astype(jnp.bfloat16), 'seq')  12.8 us
    unnamed x18, local copies, waits for them, and re-layouts  7.49 us
    ppermute x3, starting transfers between devices, gather_around(): lax.ppermute(pieces[far - 1], axis, [(d, (d - 1) % ways) for d in range(w...  7.44 us
    dot_general x16, matrix products, step_pass(): jnp.einsum('cgrbt,btgd->cgrbd', weights, value_tile, preferred_element_ty...  5.59 us
    dot_general x16, matrix products, step_pass(): jnp.einsum('cgrd,tgd->cgrt', block_queries, key_tile, preferred_element_t...  5.24 us
  transfers between devices with their start and end apart: 5, of which 3 were waited for; matrix products, arithmetic and copies ran while one was open for 21% of the time, Pallas kernels for 0%

profile of v1, /device:TPU:0, one launch (start us, length us, event | category | flops | bytes accessed | tf_op | source)
XLA Modules:
  0.0 129.0 jit_solution(10030864608924794815)
XLA Ops:
  6.5 1.5 %copy.39 = bf16[64,256]{0,1:T(8,128)(2,1)} copy(bf16[64,256]{1,0:T(8,128)(2,1)} %param.12) | data formatting | bytes 65536 | tf_op args[1]
  8.1 5.0 %collective-permute-start = (bf16[64,256]{0,1:T(8,128)(2,1)}, bf16[64,256]{0,1:T(8,128)(2,1)S(1)}, u32[]{:S(2)}, u32[]{:S(2)}) collective-permute-start(bf16[64,256]{0,1:T(8,128)(2,1)} %copy.39), channel_id=1, source_target_pairs={{0,3},{1,0},{2,1},{3,2},{4,7},{5,4},{6,5},{7,6},{8,11},{9,8},{10,9... | collective-permute-start | bytes 98312 | tf_op jit(solution)/shard_map/ppermute | solution.py:15
  13.8 15.9 %all_gather.6 = bf16[256,1024]{1,0:T(8,128)(2,1)S(1)} all-gather(bf16[64,1024]{1,0:T(8,128)(2,1)S(1)} %copy-done), channel_id=1, replica_groups=mesh['group'=2,'head'=4,'seq'=4] {'seq'}, dimensions={0}, use_global_device_ids=true | all-gather | bytes 655360 | tf_op jit(solution)/shard_map/all_gather | solution.py:36
  31.2 1.3 copy.32
  32.8 18.3 %while.29 = (s32[]{:T(128)}, f32[4,64,2,4]{1,0,3,2:T(4,128)S(1)}, f32[4,64,2,4,128]{4,3,2,1,0:T(4,128)S(1)}, f32[4,64,2,4]{1,0,3,2:T(4,128)S(1)}, bf16[4,64,2,4,...) while((s32[]{:T(128)}, f32[4,64,2,4]{1,0,3,2:T(4,128)S(1)}, ...), condition=%wide.region_5.6_spmd, body=%wide.region_0.5_spmd.sunk | while | flops 68749824 | bytes 3850228 | solution.py:96
  32.9 4.1 %while.30 = (s32[]{:T(128)}, f32[64,2,4]{0,2,1:T(4,128)S(1)}, f32[64,2,4,128]{3,0,2,1:T(8,128)S(1)}, f32[64,2,4]{0,2,1:T(4,128)S(1)}, s32[]{:T(128)}, /*index=5*...) while((s32[]{:T(128)}, f32[64,2,4]{0,2,1:T(4,128)S(1)}, ...), condition=%wide.region_4.4_spmd, body=%wide.region_1.3_spmd.sunk | while | flops 68749824 | bytes 2526915 | solution.py:94
  37.5 4.1 %while.30 = (s32[]{:T(128)}, f32[64,2,4]{0,2,1:T(4,128)S(1)}, f32[64,2,4,128]{3,0,2,1:T(8,128)S(1)}, f32[64,2,4]{0,2,1:T(4,128)S(1)}, s32[]{:T(128)}, /*index=5*...) while((s32[]{:T(128)}, f32[64,2,4]{0,2,1:T(4,128)S(1)}, ...), condition=%wide.region_4.4_spmd, body=%wide.region_1.3_spmd.sunk | while | flops 68749824 | bytes 2526915 | solution.py:94
  42.0 4.1 %while.30 = (s32[]{:T(128)}, f32[64,2,4]{0,2,1:T(4,128)S(1)}, f32[64,2,4,128]{3,0,2,1:T(8,128)S(1)}, f32[64,2,4]{0,2,1:T(4,128)S(1)}, s32[]{:T(128)}, /*index=5*...) while((s32[]{:T(128)}, f32[64,2,4]{0,2,1:T(4,128)S(1)}, ...), condition=%wide.region_4.4_spmd, body=%wide.region_1.3_spmd.sunk | while | flops 68749824 | bytes 2526915 | solution.py:94
  46.6 4.1 %while.30 = (s32[]{:T(128)}, f32[64,2,4]{0,2,1:T(4,128)S(1)}, f32[64,2,4,128]{3,0,2,1:T(8,128)S(1)}, f32[64,2,4]{0,2,1:T(4,128)S(1)}, s32[]{:T(128)}, /*index=5*...) while((s32[]{:T(128)}, f32[64,2,4]{0,2,1:T(4,128)S(1)}, ...), condition=%wide.region_4.4_spmd, body=%wide.region_1.3_spmd.sunk | while | flops 68749824 | bytes 2526915 | solution.py:94
  51.9 3.5 %collective-permute-done.1 = bf16[64,256]{0,1:T(8,128)(2,1)S(1)} collective-permute-done((bf16[64,256]{0,1:T(8,128)(2,1)S(1)}, bf16[64,256]{0,1:T(8,128)(2,1)S(1)}, u32[]{:S(2)}, u32[]{:S(2)}) %collective-permute-start.1) | collective-permute-done | bytes 32800 | tf_op jit(solution)/shard_map/ppermute | solution.py:15
  55.3 2.3 %collective-permute-start.2 = (bf16[64,256]{0,1:T(8,128)(2,1)S(1)}, bf16[64,256]{0,1:T(8,128)(2,1)S(1)}, u32[]{:S(2)}, u32[]{:S(2)}) collective-permute-start(bf16[64,256]{0,1:T(8,128)(2,1)S(1)} %collective-permute-done.1), channel_id=1, source_target_pairs={{0,3},{1,0},{2,1},{3,2},{4,7},{5,4},{6,5},{7,6},{8,11},{9,8},{10,9... | collective-permute-start | bytes 98312 | tf_op jit(solution)/shard_map/ppermute | solution.py:15
  58.5 1.1 collective-permute-done.2
  59.7 1.1 concatenate.6
  61.4 12.8 %pmax.7 = bf16[256,8]{0,1:T(8,128)(2,1)S(1)} all-reduce(bf16[256,8]{0,1:T(8,128)(2,1)S(1)} %convert_element_type.27), channel_id=1, replica_groups=mesh['group'=2,'head'=4,'seq'=4] {'seq'}, use_global_device_ids=true, to_apply=%region_7.8 | all-reduce | flops 2048 | bytes 8192 | tf_op jit(solution)/shard_map/pmax | solution.py:126
  74.3 0.8 copy.58
  75.3 1.6 %mul.75 = f32[256,2,4,128]{3,2,1,0:T(4,128)} broadcast(f32[256,2,4]{2,1,0:T(2,128)S(1)} %copy.43), dimensions={0,1,2} | broadcast | bytes 1056768 | tf_op jit(solution)/shard_map/mul | solution.py:131
  76.9 1.6 %mul.76 = f32[256,1024]{1,0:T(8,128)S(1)} reshape(f32[256,2,4,128]{3,2,1,0:T(4,128)} %mul.75) | data formatting | bytes 2097152 | tf_op jit(solution)/shard_map/mul | solution.py:131
  78.6 1.2 mul.77
  79.8 0.7 copy-done.4
  80.5 13.5 %all_gather.7 = bf16[256,256]{1,0:T(8,128)(2,1)S(1)} all-gather(bf16[64,256]{1,0:T(8,128)(2,1)S(1)} %copy-done.4), channel_id=1, replica_groups=mesh['group'=2,'head'=4,'seq'=4] {'seq'}, dimensions={0}, use_global_device_ids=true | all-gather | bytes 163840 | tf_op jit(solution)/shard_map/all_gather | solution.py:38
  95.1 0.8 copy.59
  96.0 24.4 %reduce-scatter.5.cloned.1.call-done = f32[64,1024]{1,0:T(8,128)} async-done(((f32[256,1024]{1,0:T(8,128)}), f32[64,1024]{1,0:T(8,128)}) %reduce-scatter.5.cloned.1.call-update) | async-done | bytes 262160 | tf_op jit(solution)/shard_map/reduce_scatter | solution.py:134
  120.6 0.8 copy-done.3
  121.4 0.7 fusion.13
  (164 shorter events, 22.8 us)
Async XLA Ops:
  6.5 7.2 %copy-start = (bf16[64,1024]{1,0:T(8,128)(2,1)S(1)}, bf16[64,1024]{1,0:T(8,128)(2,1)}, u32[]{:S(2)}) copy-start(bf16[64,1024]{1,0:T(8,128)(2,1)} %param.11) | copy-start | bytes 393220
  6.5 88.6 %reduce-scatter.7.cloned.1.call-start = ((), (), s32[]{:S(2)}) async-start(), calls=%async_computation.3 | async-start | bytes 163840
  8.1 43.0 %collective-permute-start = (bf16[64,256]{0,1:T(8,128)(2,1)}, bf16[64,256]{0,1:T(8,128)(2,1)S(1)}, u32[]{:S(2)}, u32[]{:S(2)}) collective-permute-start(bf16[64,256]{0,1:T(8,128)(2,1)} %copy.39), channel_id=1, source_target_pairs={{0,3},{1,0},{2,1},{3,2},{4,7},{5,4},{6,5},{7,6},{8,11},{9,8},{10,9... | collective-permute-start | bytes 98312 | tf_op jit(solution)/shard_map/ppermute | solution.py:15
  29.7 1.0 copy-start.2
  32.7 25.2 %copy-start.1 = (bf16[64,1024]{1,0:T(8,128)(2,1)S(1)}, bf16[64,1024]{1,0:T(8,128)(2,1)}, u32[]{:S(2)}) copy-start(bf16[64,1024]{1,0:T(8,128)(2,1)} %param.11) | copy-start | bytes 393220
  51.0 4.3 %collective-permute-start.1 = (bf16[64,256]{0,1:T(8,128)(2,1)S(1)}, bf16[64,256]{0,1:T(8,128)(2,1)S(1)}, u32[]{:S(2)}, u32[]{:S(2)}) collective-permute-start(bf16[64,256]{0,1:T(8,128)(2,1)S(1)} %collective-permute-done), channel_id=1, source_target_pairs={{0,3},{1,0},{2,1},{3,2},{4,7},{5,4},{6,5},{7,6},{8,11},{9,8},{10,9... | collective-permute-start | bytes 98312 | tf_op jit(solution)/shard_map/ppermute | solution.py:15
  51.1 0.7 copy-start.5
  55.3 4.3 %collective-permute-start.2 = (bf16[64,256]{0,1:T(8,128)(2,1)S(1)}, bf16[64,256]{0,1:T(8,128)(2,1)S(1)}, u32[]{:S(2)}, u32[]{:S(2)}) collective-permute-start(bf16[64,256]{0,1:T(8,128)(2,1)S(1)} %collective-permute-done.1), channel_id=1, source_target_pairs={{0,3},{1,0},{2,1},{3,2},{4,7},{5,4},{6,5},{7,6},{8,11},{9,8},{10,9... | collective-permute-start | bytes 98312 | tf_op jit(solution)/shard_map/ppermute | solution.py:15
  75.1 45.4 %reduce-scatter.5.cloned.1.call-start = ((), (), s32[]{:S(2)}) async-start(), calls=%async_computation.2 | async-start | bytes 1310720 | tf_op jit(solution)/shard_map/reduce_scatter | solution.py:134
  79.8 0.8 copy-start.4
  120.4 0.9 copy-start.3
Sparse Core Ops, SparseCore 0:
  75.2 17.4 reduce-scatter.6
  95.1 25.3 reduce-scatter.4
